TPU v7x, 512 devices: a whole 4x8x8 slice. The times are simulated.
512 devices in a mesh: seq: 16 (over z, core), mlp: 8 (over y), tp: 4 (over x).
Axes of the slice: x: 4, y: 8, z: 8, core: 2. Of those that a mesh axis runs over, the one named last changes fastest.
Arguments:
- hidden: bfloat16 [64, 2048], P('mlp'), may hold values from -6 to 6
- lengths: int32 [64], P('mlp'), may hold values from 4 to 8192, as said below
- attention_gain: bfloat16 [2048], replicated, may hold values from 0.099609375 to 1.8984375
- query_weight: bfloat16 [2048, 2048], P('seq', 'tp'), may hold values from -0.125 to 0.125
- key_weight: bfloat16 [2048, 512], P('seq', 'tp'), may hold values from -0.125 to 0.125
- value_weight: bfloat16 [2048, 512], P('seq', 'tp'), may hold values from -0.125 to 0.125
- cached_keys: bfloat16 [64, 8192, 512], P('mlp', 'seq', 'tp'), may hold values from -800 to 800
- cached_values: bfloat16 [64, 8192, 512], P('mlp', 'seq', 'tp'), may hold values from -8 to 8
- output_weight: bfloat16 [2048, 2048], P('tp', 'seq'), may hold values from -0.125 to 0.125
- feedforward_gain: bfloat16 [2048], replicated, may hold values from 0.099609375 to 1.8984375
- gate_weight: bfloat16 [2048, 8192], P('mlp', ('seq', 'tp')), may hold values from -0.125 to 0.125
- up_weight: bfloat16 [2048, 8192], P('mlp', ('seq', 'tp')), may hold values from -0.125 to 0.125
- down_weight: bfloat16 [8192, 2048], P(('seq', 'tp'), 'mlp'), may hold values from -0.0625 to 0.0625
Outputs:
- updated_hidden: bfloat16 [64, 2048], P('mlp')
- new_keys: bfloat16 [64, 512], P('mlp', 'tp')
- new_values: bfloat16 [64, 512], P('mlp', 'tp')
Inputs may be any that keep to these rules, and one draw needn't show every extreme that they name: `lengths`: one request in every draw has exactly 8192 cached tokens.
All inputs are finite; a program needn't handle non-finite values.
Results may differ from a plain program's by a relative error of at most 0.012.
Values may be sent and summed in bfloat16 or wider, within the bound.
No kernel may reach another device: no remote copies, remote signals or barrier semaphores. Data moves between devices by JAX's collectives and lax.ppermute only.
A program may use at most 64 MiB of HBM per device.

v0:
```python
import jax
import jax.numpy as jnp
from jax import lax
from jax.sharding import PartitionSpec as P

HD = 64


def rms_norm(vectors, weights):
    mean_square = jnp.mean(vectors * vectors, axis=-1, keepdims=True)
    return vectors * lax.rsqrt(mean_square + 1e-05) * weights.astype(jnp.float32)


def rotate(vectors, positions):
    half_dim = vectors.shape[-1] // 2
    inverse = 500000.0 ** (-(jnp.arange(half_dim, dtype=jnp.float32) * 2.0 / vectors.shape[-1]))
    angles = positions.astype(jnp.float32)[:, None] * inverse[None, :]
    cosine = jnp.cos(angles)[:, None, :]
    sine_part = jnp.sin(angles)[:, None, :]
    first_half = vectors[..., :half_dim]
    second_half = vectors[..., half_dim:]
    return jnp.concatenate(
        [
            first_half * cosine - second_half * sine_part,
            second_half * cosine + first_half * sine_part,
        ],
        axis=-1,
    )


def gathered_sum(x, axis):
    return jnp.sum(lax.all_gather(x, axis), axis=0)


def gather_blocks(x, axis):
    size = lax.axis_size(axis)
    me = lax.axis_index(axis)
    held = x[None]
    step = 1
    while step < size:
        other = lax.ppermute(held, axis, [(i, i ^ step) for i in range(size)])
        upper = me // step % 2 == 1
        held = jnp.where(
            upper, jnp.concatenate([other, held], axis=0), jnp.concatenate([held, other], axis=0)
        )
        step *= 2
    return held


def butterfly_sum(x, axis):
    size = lax.axis_size(axis)
    step = 1
    while step < size:
        pairs = [(i, i ^ step) for i in range(size)]
        x = x + lax.ppermute(x, axis, pairs)
        step *= 2
    return x


def per_device(
    hidden,
    lengths,
    attention_gain,
    query_weight,
    key_weight,
    value_weight,
    cached_keys,
    cached_values,
    output_weight,
    feedforward_gain,
    gate_weight,
    up_weight,
    down_weight,
):
    slab_rows, hidden_units = gate_weight.shape
    with jax.named_scope("mlp_weight_gather"):
        slab = jnp.stack(
            [gate_weight, up_weight, down_weight.reshape(slab_rows, hidden_units)], axis=0
        )
        blocks = gather_blocks(slab, "mlp")
    slabs = blocks.shape[0]
    gate_full = blocks[:, 0].reshape(slabs * slab_rows, hidden_units)
    up_full = blocks[:, 1].reshape(slabs * slab_rows, hidden_units)
    down_blocks = blocks[:, 2].reshape(slabs, hidden_units, slab_rows)
    requests = hidden.shape[0]
    stream = hidden.astype(jnp.float32)
    normed = rms_norm(stream, attention_gain).astype(jnp.bfloat16)
    column_width = query_weight.shape[0]
    own_columns = lax.dynamic_slice_in_dim(
        normed, lax.axis_index("seq") * column_width, column_width, 1
    )
    query_width = query_weight.shape[1]
    key_width = key_weight.shape[1]
    with jax.named_scope("qkv_projection"):
        partial = jnp.concatenate(
            [
                jnp.dot(own_columns, query_weight, preferred_element_type=jnp.float32),
                jnp.dot(own_columns, key_weight, preferred_element_type=jnp.float32),
                jnp.dot(own_columns, value_weight, preferred_element_type=jnp.float32),
            ],
            axis=1,
        )
        total = gathered_sum(partial, "seq")
    queries_raw = total[:, :query_width]
    keys_raw = total[:, query_width : query_width + key_width]
    values_raw = total[:, query_width + key_width :]
    local_heads = query_width // HD
    key_heads = key_width // HD
    group_size = local_heads // key_heads
    queries = rotate(queries_raw.reshape(requests, local_heads, HD), lengths).astype(jnp.bfloat16)
    new_keys = (
        rotate(keys_raw.reshape(requests, key_heads, HD), lengths)
        .reshape(requests, key_heads * HD)
        .astype(jnp.bfloat16)
    )
    new_values = values_raw.astype(jnp.bfloat16)
    grouped = queries.reshape(requests, key_heads, group_size, HD)
    block_span = cached_keys.shape[1]
    key_blocks = cached_keys.reshape(requests, block_span, key_heads, HD)
    value_blocks = cached_values.reshape(requests, block_span, key_heads, HD)
    score_scale = HD ** (-0.5)
    first_position = lax.axis_index("seq") * block_span
    positions = first_position + jnp.arange(block_span, dtype=jnp.int32)
    valid_mask = (positions[None, :] < lengths[:, None])[:, None, None, :]
    with jax.named_scope("local_attention"):
        scores = (
            jnp.einsum("rgqd,rpgd->rgqp", grouped, key_blocks, preferred_element_type=jnp.float32)
            * score_scale
        )
        block_max = jnp.max(jnp.where(valid_mask, scores, -1e30), axis=-1)
        exp_weights = jnp.where(valid_mask, jnp.exp(scores - block_max[..., None]), 0.0)
        block_sum = jnp.sum(exp_weights, axis=-1)
        block_acc = jnp.einsum(
            "rgqp,rpgd->rgqd",
            exp_weights.astype(jnp.bfloat16),
            value_blocks,
            preferred_element_type=jnp.float32,
        )
    with jax.named_scope("softmax_merge"):
        state = jnp.concatenate([block_max[..., None], block_sum[..., None], block_acc], axis=-1)
        every_state = lax.all_gather(state, "seq")
        every_max = every_state[..., 0]
        every_sum = every_state[..., 1]
        every_acc = every_state[..., 2:]
        query_float = grouped.astype(jnp.float32)
        self_score = (
            jnp.sum(
                query_float * new_keys.astype(jnp.float32).reshape(requests, key_heads, 1, HD),
                axis=-1,
            )
            * score_scale
        )
        overall_max = jnp.maximum(jnp.max(every_max, axis=0), self_score)
        rescale = jnp.exp(every_max - overall_max[None])
        self_weight = jnp.exp(self_score - overall_max)
        total_weight = jnp.sum(every_sum * rescale, axis=0) + self_weight
        weighted_sum = jnp.sum(every_acc * rescale[..., None], axis=0) + self_weight[
            ..., None
        ] * new_values.astype(jnp.float32).reshape(requests, key_heads, 1, HD)
        attended = (
            (weighted_sum / total_weight[..., None])
            .reshape(requests, local_heads * HD)
            .astype(jnp.bfloat16)
        )
    with jax.named_scope("output_projection"):
        partial_output = jnp.dot(attended, output_weight, preferred_element_type=jnp.float32)
        projected = lax.psum(partial_output, "tp").astype(jnp.bfloat16)
        projected = lax.all_gather(projected, "seq", axis=1, tiled=True)
    mixed_stream = stream + projected.astype(jnp.float32)
    mlp_input = rms_norm(mixed_stream, feedforward_gain).astype(jnp.bfloat16)
    with jax.named_scope("feed_forward"):
        gate = jnp.dot(mlp_input, gate_full, preferred_element_type=jnp.float32)
        upward = jnp.dot(mlp_input, up_full, preferred_element_type=jnp.float32)
        activated = (jax.nn.silu(gate) * upward).astype(jnp.bfloat16)
        down_part = jnp.einsum(
            "rh,jhc->rjc", activated, down_blocks, preferred_element_type=jnp.float32
        ).reshape(requests, slabs * slab_rows)
    with jax.named_scope("down_reduction"):
        down_total = butterfly_sum(gathered_sum(down_part, "tp"), "seq").astype(jnp.bfloat16)
    updated_hidden = (mixed_stream + down_total.astype(jnp.float32)).astype(jnp.bfloat16)
    return (updated_hidden, new_keys, new_values)


def solution(mesh):
    return jax.shard_map(
        per_device,
        mesh=mesh,
        in_specs=(
            P("mlp", None),
            P("mlp"),
            P(),
            P("seq", "tp"),
            P("seq", "tp"),
            P("seq", "tp"),
            P("mlp", "seq", "tp"),
            P("mlp", "seq", "tp"),
            P("tp", "seq"),
            P(),
            P("mlp", ("seq", "tp")),
            P("mlp", ("seq", "tp")),
            P(("seq", "tp"), "mlp"),
        ),
        out_specs=(P("mlp", None), P("mlp", "tp"), P("mlp", "tp")),
        check_vma=False,
    )
```

profile of v0, /device:TPU:64, one launch (start us, length us, event | category | flops | bytes accessed | tf_op | source)
XLA Modules:
  0.0 163.4 jit_solution(15652032731097320502)
XLA Ops:
  0.7 1.0 reshape.177
  1.6 0.9 maximum_bitcast_fusion
  2.5 3.5 %collective-permute-start = (bf16[1,3,256,128]{3,2,1,0:T(8,128)(2,1)S(1)}, bf16[1,3,256,128]{3,2,1,0:T(8,128)(2,1)}, u32[]{:S(2)}, u32[]{:S(2)}) collective-permute-start(bf16[1,3,256,128]{3,2,1,0:T(8,128)(2,1)S(1)} %maximum_bitcast_fusion), channel_id=1, source_target_pairs={{0,4},{4,0},{8,12},{12,8},{16,20},{20,16},{24,28},{28,24},{1,5},{5... | collective-permute-start | bytes 589832 | tf_op jit(solution)/shard_map/mlp_weight_gather/ppermute | solution.py:41
  6.0 0.8 convert_element_type.70
  6.8 0.9 multiply_reduce_fusion.1
  7.7 0.8 dynamic-slice
  8.5 0.2 fusion.26
  8.7 0.9 fusion.24
  9.6 1.0 fusion.28
  10.6 21.2 %all-gather = f32[128,768]{1,0:T(8,128)S(1)} all-gather(f32[8,768]{1,0:T(8,128)S(1)} %pad_maximum_fusion.1), channel_id=2, replica_groups=mesh['seq'=16,'mlp'=8,'tp'=4] {'seq'}, dimensions={0}, use_global_device_ids=true | all-gather | bytes 417792 | tf_op jit(solution)/shard_map/qkv_projection/all_gather | solution.py:32
  32.0 0.5 copy.107
  32.6 0.5 copy.110
  33.3 0.4 select_reduce_fusion
  33.7 0.2 fusion.2
  34.0 0.4 fusion.3
  34.4 0.2 copy.112
  34.6 0.2 copy.111
  34.9 18.2 %all-gather.1 = f32[128,2,4,66]{3,2,1,0:T(4,128)S(1)} all-gather(f32[8,2,4,66]{3,2,1,0:T(4,128)S(1)} %pad_maximum_fusion), channel_id=3, replica_groups=mesh['seq'=16,'mlp'=8,'tp'=4] {'seq'}, dimensions={0}, use_global_device_ids=true | all-gather | bytes 287232 | tf_op jit(solution)/shard_map/softmax_merge/all_gather | solution.py:141
  53.3 0.3 fusion.23
  53.5 0.3 slice-done
  54.1 0.2 multiply_reduce_fusion.2
  54.4 0.5 copy.119
  54.8 0.5 copy.127
  55.4 1.1 maximum_select_fusion.2
  56.6 4.5 %collective-permute-start.1 = (bf16[2,3,256,128]{3,2,1,0:T(8,128)(2,1)S(1)}, bf16[2,3,256,128]{3,2,1,0:T(8,128)(2,1)S(1)}, u32[]{:S(2)}, u32[]{:S(2)}) collective-permute-start(bf16[2,3,256,128]{3,2,1,0:T(8,128)(2,1)S(1)} %maximum_select_fusion.2), channel_id=1, source_target_pairs={{0,8},{4,12},{8,0},{12,4},{16,24},{20,28},{24,16},{28,20},{1,9},{5... | collective-permute-start | bytes 1179656 | tf_op jit(solution)/shard_map/mlp_weight_gather/ppermute | solution.py:41
  61.1 0.2 fusion.10
  61.5 0.3 fusion
  61.8 17.2 %collective-permute-done.1 = bf16[2,3,256,128]{3,2,1,0:T(8,128)(2,1)S(1)} collective-permute-done((bf16[2,3,256,128]{3,2,1,0:T(8,128)(2,1)S(1)}, bf16[2,3,256,128]{3,2,1,0:T(8,128)(2,1)S(1)}, u32[]{:S(2)}, u32[]{:S(2)}) %collective-permute-start.1) | collective-permute-done | bytes 393248 | tf_op jit(solution)/shard_map/mlp_weight_gather/ppermute | solution.py:41
  79.2 6.9 %collective-permute-start.2 = (bf16[4,3,256,128]{3,2,1,0:T(8,128)(2,1)S(1)}, bf16[4,3,256,128]{3,2,1,0:T(8,128)(2,1)S(1)}, u32[]{:S(2)}, u32[]{:S(2)}) collective-permute-start(bf16[4,3,256,128]{3,2,1,0:T(8,128)(2,1)S(1)} %maximum_select_fusion.1), channel_id=1, source_target_pairs={{0,16},{4,20},{8,24},{12,28},{16,0},{20,4},{24,8},{28,12},{1,17},{... | collective-permute-start | bytes 2359304 | tf_op jit(solution)/shard_map/mlp_weight_gather/ppermute | solution.py:41
  86.5 10.5 %psum.7 = bf16[8,128]{1,0:T(8,128)(2,1)S(1)} all-reduce(f32[8,128]{1,0:T(8,128)S(1)} %fusion.30), channel_id=1, replica_groups=mesh['seq'=16,'mlp'=8,'tp'=4] {'tp'}, use_global_device_ids=true, to_apply=%region_8.9 | all-reduce | flops 1024 | bytes 6144 | tf_op jit(solution)/shard_map/output_projection/psum | solution.py:167
  96.9 14.5 %all_gather.22 = bf16[8,2048]{1,0:T(8,128)(2,1)S(1)} all-gather(bf16[8,128]{1,0:T(8,128)(2,1)S(1)} %psum.7), channel_id=1, replica_groups=mesh['seq'=16,'mlp'=8,'tp'=4] {'seq'}, dimensions={1}, use_global_device_ids=true | all-gather | bytes 34816 | tf_op jit(solution)/shard_map/output_projection/all_gather | solution.py:168
  111.6 9.9 %collective-permute-done.2 = bf16[4,3,256,128]{3,2,1,0:T(8,128)(2,1)S(1)} collective-permute-done((bf16[4,3,256,128]{3,2,1,0:T(8,128)(2,1)S(1)}, bf16[4,3,256,128]{3,2,1,0:T(8,128)(2,1)S(1)}, u32[]{:S(2)}, u32[]{:S(2)}) %collective-permute-start.2) | collective-permute-done | bytes 786464 | tf_op jit(solution)/shard_map/mlp_weight_gather/ppermute | solution.py:41
  121.5 0.2 maximum_select_fusion
  121.9 0.2 reshape_squeeze.11
  122.0 0.3 copy.121
  122.3 0.2 fusion.19
  122.6 0.4 fusion.13
  123.0 12.6 %all-gather.2 = f32[32,2048]{1,0:T(8,128)S(1)} all-gather(f32[8,2048]{1,0:T(8,128)S(1)} %fusion.13), channel_id=4, replica_groups=mesh['seq'=16,'mlp'=8,'tp'=4] {'tp'}, dimensions={0}, use_global_device_ids=true | all-gather | bytes 327680 | tf_op jit(solution)/shard_map/down_reduction/all_gather | solution.py:32
  135.6 1.9 %collective-permute-start.3 = (f32[8,2048]{1,0:T(8,128)S(1)}, f32[8,2048]{1,0:T(8,128)S(1)}, u32[]{:S(2)}, u32[]{:S(2)}) collective-permute-start(f32[8,2048]{1,0:T(8,128)S(1)} %bitcast_reduce_fusion.1), channel_id=1, source_target_pairs={{0,32},{32,0},{64,96},{96,64},{128,160},{160,128},{192,224},{224,1... | collective-permute-start | bytes 196616 | tf_op jit(solution)/shard_map/down_reduction/ppermute | solution.py:55
  137.6 1.2 collective-permute-done.3
  138.8 2.3 %collective-permute-start.4 = (f32[8,2048]{1,0:T(8,128)S(1)}, f32[8,2048]{1,0:T(8,128)S(1)}, u32[]{:S(2)}, u32[]{:S(2)}) collective-permute-start(f32[8,2048]{1,0:T(8,128)S(1)} %add.98), channel_id=1, source_target_pairs={{0,64},{32,96},{64,0},{96,32},{128,192},{160,224},{192,128},{224,1... | collective-permute-start | bytes 196616 | tf_op jit(solution)/shard_map/down_reduction/ppermute | solution.py:55
  141.1 3.9 %collective-permute-done.4 = f32[8,2048]{1,0:T(8,128)S(1)} collective-permute-done((f32[8,2048]{1,0:T(8,128)S(1)}, f32[8,2048]{1,0:T(8,128)S(1)}, u32[]{:S(2)}, u32[]{:S(2)}) %collective-permute-start.4) | collective-permute-done | bytes 65568 | tf_op jit(solution)/shard_map/down_reduction/ppermute | solution.py:55
  145.0 2.2 %collective-permute-start.5 = (f32[8,2048]{1,0:T(8,128)S(1)}, f32[8,2048]{1,0:T(8,128)S(1)}, u32[]{:S(2)}, u32[]{:S(2)}) collective-permute-start(f32[8,2048]{1,0:T(8,128)S(1)} %add.99), channel_id=1, source_target_pairs={{0,128},{32,160},{64,192},{96,224},{128,0},{160,32},{192,64},{224,... | collective-permute-start | bytes 196616 | tf_op jit(solution)/shard_map/down_reduction/ppermute | solution.py:55
  147.1 4.9 %collective-permute-done.5 = f32[8,2048]{1,0:T(8,128)S(1)} collective-permute-done((f32[8,2048]{1,0:T(8,128)S(1)}, f32[8,2048]{1,0:T(8,128)S(1)}, u32[]{:S(2)}, u32[]{:S(2)}) %collective-permute-start.5) | collective-permute-done | bytes 65568 | tf_op jit(solution)/shard_map/down_reduction/ppermute | solution.py:55
  152.0 3.4 %collective-permute-start.6 = (f32[8,2048]{1,0:T(8,128)S(1)}, f32[8,2048]{1,0:T(8,128)S(1)}, u32[]{:S(2)}, u32[]{:S(2)}) collective-permute-start(f32[8,2048]{1,0:T(8,128)S(1)} %add.100), channel_id=1, source_target_pairs={{0,256},{32,288},{64,320},{96,352},{128,384},{160,416},{192,448},{... | collective-permute-start | bytes 196616 | tf_op jit(solution)/shard_map/down_reduction/ppermute | solution.py:55
  155.4 0.7 convert_element_type.88
  156.1 6.7 %collective-permute-done.6 = f32[8,2048]{1,0:T(8,128)S(1)} collective-permute-done((f32[8,2048]{1,0:T(8,128)S(1)}, f32[8,2048]{1,0:T(8,128)S(1)}, u32[]{:S(2)}, u32[]{:S(2)}) %collective-permute-start.6) | collective-permute-done | bytes 65568 | tf_op jit(solution)/shard_map/down_reduction/ppermute | solution.py:55
  162.8 0.6 add_convert_fusion
  (59 shorter events, 2.0 us)
Async XLA Ops:
  0.6 7.8 %copy-start = (bf16[128,512]{1,0:T(8,128)(2,1)S(1)}, bf16[128,512]{1,0:T(8,128)(2,1)}, u32[]{:S(2)}) copy-start(bf16[128,512]{1,0:T(8,128)(2,1)} %param.16) | copy-start | bytes 393220
  0.6 31.3 %copy-start.9 = (s32[8]{0:T(128)S(1)}, s32[8]{0:T(128)}, u32[]{:S(2)}) copy-start(s32[8]{0:T(128)} %param.14) | copy-start | bytes 100
  0.7 31.4 %copy-start.2 = (bf16[8,512,128]{2,1,0:T(8,128)(2,1)S(1)}, bf16[8,512,128]{2,1,0:T(8,128)(2,1)}, u32[]{:S(2)}) copy-start(bf16[8,512,128]{2,1,0:T(8,128)(2,1)} %param.19) | copy-start | bytes 3145732
  2.5 52.9 %collective-permute-start = (bf16[1,3,256,128]{3,2,1,0:T(8,128)(2,1)S(1)}, bf16[1,3,256,128]{3,2,1,0:T(8,128)(2,1)}, u32[]{:S(2)}, u32[]{:S(2)}) collective-permute-start(bf16[1,3,256,128]{3,2,1,0:T(8,128)(2,1)S(1)} %maximum_bitcast_fusion), channel_id=1, source_target_pairs={{0,4},{4,0},{8,12},{12,8},{16,20},{20,16},{24,28},{28,24},{1,5},{5... | collective-permute-start | bytes 589832 | tf_op jit(solution)/shard_map/mlp_weight_gather/ppermute | solution.py:41
  9.6 23.0 %copy-start.3 = (bf16[8,512,128]{2,1,0:T(8,128)(2,1)S(1)}, bf16[8,512,128]{2,1,0:T(8,128)(2,1)}, u32[]{:S(2)}) copy-start(bf16[8,512,128]{2,1,0:T(8,128)(2,1)} %param.20) | copy-start | bytes 3145732
  31.8 1.3 copy-start.5
  53.2 0.7 slice-start
  53.8 7.4 %copy-start.6 = (f32[8,768]{1,0:T(8,128)S(1)}, f32[8,768]{1,0:T(8,128)}, u32[]{:S(2)}) copy-start(f32[8,768]{1,0:T(8,128)} %copy-done.5) | copy-start | bytes 73732
  55.4 30.9 %copy-start.8 = (bf16[2048]{0:T(1024)(128)(2,1)S(1)}, bf16[2048]{0:T(1024)(128)(2,1)}, u32[]{:S(2)}) copy-start(bf16[2048]{0:T(1024)(128)(2,1)} %param.22) | copy-start | bytes 12292
  55.4 30.9 %copy-start.4 = (bf16[512,128]{1,0:T(8,128)(2,1)S(1)}, bf16[512,128]{1,0:T(8,128)(2,1)}, u32[]{:S(2)}) copy-start(bf16[512,128]{1,0:T(8,128)(2,1)} %param.21) | copy-start | bytes 393220
  56.5 54.9 %copy-start.1 = (bf16[8,2048]{1,0:T(8,128)(2,1)S(1)}, bf16[8,2048]{1,0:T(8,128)(2,1)}, u32[]{:S(2)}) copy-start(bf16[8,2048]{1,0:T(8,128)(2,1)} %param.13) | copy-start | bytes 98308
  56.6 22.5 %collective-permute-start.1 = (bf16[2,3,256,128]{3,2,1,0:T(8,128)(2,1)S(1)}, bf16[2,3,256,128]{3,2,1,0:T(8,128)(2,1)S(1)}, u32[]{:S(2)}, u32[]{:S(2)}) collective-permute-start(bf16[2,3,256,128]{3,2,1,0:T(8,128)(2,1)S(1)} %maximum_select_fusion.2), channel_id=1, source_target_pairs={{0,8},{4,12},{8,0},{12,4},{16,24},{20,28},{24,16},{28,20},{1,9},{5... | collective-permute-start | bytes 1179656 | tf_op jit(solution)/shard_map/mlp_weight_gather/ppermute | solution.py:41
  61.3 60.5 %copy-start.7 = (bf16[8,128]{1,0:T(8,128)(2,1)}, bf16[8,128]{1,0:T(8,128)(2,1)S(1)}, u32[]{:S(2)}) copy-start(bf16[8,128]{1,0:T(8,128)(2,1)S(1)} %slice.79) | copy-start | bytes 6148
  79.2 42.3 %collective-permute-start.2 = (bf16[4,3,256,128]{3,2,1,0:T(8,128)(2,1)S(1)}, bf16[4,3,256,128]{3,2,1,0:T(8,128)(2,1)S(1)}, u32[]{:S(2)}, u32[]{:S(2)}) collective-permute-start(bf16[4,3,256,128]{3,2,1,0:T(8,128)(2,1)S(1)} %maximum_select_fusion.1), channel_id=1, source_target_pairs={{0,16},{4,20},{8,24},{12,28},{16,0},{20,4},{24,8},{28,12},{1,17},{... | collective-permute-start | bytes 2359304 | tf_op jit(solution)/shard_map/mlp_weight_gather/ppermute | solution.py:41
  135.6 3.1 %collective-permute-start.3 = (f32[8,2048]{1,0:T(8,128)S(1)}, f32[8,2048]{1,0:T(8,128)S(1)}, u32[]{:S(2)}, u32[]{:S(2)}) collective-permute-start(f32[8,2048]{1,0:T(8,128)S(1)} %bitcast_reduce_fusion.1), channel_id=1, source_target_pairs={{0,32},{32,0},{64,96},{96,64},{128,160},{160,128},{192,224},{224,1... | collective-permute-start | bytes 196616 | tf_op jit(solution)/shard_map/down_reduction/ppermute | solution.py:55
  138.8 6.2 %collective-permute-start.4 = (f32[8,2048]{1,0:T(8,128)S(1)}, f32[8,2048]{1,0:T(8,128)S(1)}, u32[]{:S(2)}, u32[]{:S(2)}) collective-permute-start(f32[8,2048]{1,0:T(8,128)S(1)} %add.98), channel_id=1, source_target_pairs={{0,64},{32,96},{64,0},{96,32},{128,192},{160,224},{192,128},{224,1... | collective-permute-start | bytes 196616 | tf_op jit(solution)/shard_map/down_reduction/ppermute | solution.py:55
  145.0 7.1 %collective-permute-start.5 = (f32[8,2048]{1,0:T(8,128)S(1)}, f32[8,2048]{1,0:T(8,128)S(1)}, u32[]{:S(2)}, u32[]{:S(2)}) collective-permute-start(f32[8,2048]{1,0:T(8,128)S(1)} %add.99), channel_id=1, source_target_pairs={{0,128},{32,160},{64,192},{96,224},{128,0},{160,32},{192,64},{224,... | collective-permute-start | bytes 196616 | tf_op jit(solution)/shard_map/down_reduction/ppermute | solution.py:55
  152.0 10.8 %collective-permute-start.6 = (f32[8,2048]{1,0:T(8,128)S(1)}, f32[8,2048]{1,0:T(8,128)S(1)}, u32[]{:S(2)}, u32[]{:S(2)}) collective-permute-start(f32[8,2048]{1,0:T(8,128)S(1)} %add.100), channel_id=1, source_target_pairs={{0,256},{32,288},{64,320},{96,352},{128,384},{160,416},{192,448},{... | collective-permute-start | bytes 196616 | tf_op jit(solution)/shard_map/down_reduction/ppermute | solution.py:55
where the time goes:
time: 164 us; the launch traced here: 163 us
  blocking collectives  77 us (47%)
  waiting for transfers between devices  43.8 us (27%)
  starting transfers between devices  24.6 us (15%)
  other arithmetic  6.82 us (4%)
  local copies, waits for them, and re-layouts  6.29 us (4%)
  matrix products  3.79 us (2%)
    all_gather x2, blocking collectives, gathered_sum(): return jnp.sum(lax.all_gather(x, axis), axis=0)  33.8 us
    ppermute x3, waiting for transfers between devices, gather_blocks(): other = lax.ppermute(held, axis, [(i, i ^ step) for i in range(size)])  27.1 us
    all_gather x1, blocking collectives, per_device(): every_state = lax.all_gather(state, 'seq')  18.2 us
    ppermute x4, waiting for transfers between devices, butterfly_sum(): x = x + lax.ppermute(x, axis, pairs)  16.8 us
    ppermute x3, starting transfers between devices, gather_blocks(): other = lax.ppermute(held, axis, [(i, i ^ step) for i in range(size)])  14.9 us
    all_gather x1, blocking collectives, per_device(): projected = lax.all_gather(projected, 'seq', axis=1, tiled=True)  14.5 us
    psum x1, blocking collectives, per_device(): projected = lax.psum(partial_output, 'tp').astype(jnp.bfloat16)  10.5 us
    ppermute x4, starting transfers between devices, butterfly_sum(): x = x + lax.ppermute(x, axis, pairs)  9.69 us
  transfers between devices with their start and end apart: 7, of which 6 were waited for; matrix products, arithmetic and copies ran while one was open for 7% of the time, Pallas kernels for 0%

commit v1 on v0

--- a/solution.py
+++ b/solution.py
@@ -4,6 +4,11 @@
 from jax.sharding import PartitionSpec as P
 
 HD = 64
+
+
+def gather_from_all(x, axis, dim):
+    copies = jnp.concatenate([x] * lax.axis_size(axis), axis=dim)
+    return lax.all_to_all(copies, axis, dim, dim, tiled=True)
 
 
 def rms_norm(vectors, weights):
@@ -165,7 +170,7 @@
     with jax.named_scope("output_projection"):
         partial_output = jnp.dot(attended, output_weight, preferred_element_type=jnp.float32)
         projected = lax.psum(partial_output, "tp").astype(jnp.bfloat16)
-        projected = lax.all_gather(projected, "seq", axis=1, tiled=True)
+        projected = gather_from_all(projected, "seq", 1)
     mixed_stream = stream + projected.astype(jnp.float32)
     mlp_input = rms_norm(mixed_stream, feedforward_gain).astype(jnp.bfloat16)
     with jax.named_scope("feed_forward"):

time: 164 us -> 178 us (1.085)
  waiting for transfers between devices: 43.8 us -> 59.5 us
  blocking collectives: 77 us -> 62.3 us
  local copies, waits for them, and re-layouts: 6.29 us -> 15.6 us
  starting transfers between devices: 24.6 us -> 28.3 us
    all_gather x1 -> x0, blocking collectives: 14.5 us -> none  [per_device(): projected = lax.all_gather(projected, 'seq', axis=1, tiled=True)]
    ppermute x3, waiting for transfers between devices: 27.1 us -> 36.4 us  [gather_blocks(): other = lax.ppermute(held, axis, [(i, i ^ step) for i in range(size)])]
    unnamed x23 -> x36, local copies, waits for them, and re-layouts: 1.58 us -> 10.3 us
    all_to_all x0 -> x1, waiting for transfers between devices: none -> 6.34 us  [gather_from_all(): return lax.all_to_all(copies, axis, dim, dim, tiled=True)]
    all_to_all x0 -> x1, starting transfers between devices: none -> 3.64 us  [gather_from_all(): return lax.all_to_all(copies, axis, dim, dim, tiled=True)]
  transfers between devices with their start and end apart: 7 -> 8, of which waited for: 6 -> 7; matrix products, arithmetic and copies ran while one was open for 7% -> 12% of each run, Pallas kernels for 0% -> 0%
where the time goes in v1:
time: 178 us; the launch traced here: 177 us
  blocking collectives  62.3 us (35%)
  waiting for transfers between devices  59.5 us (33%)
  starting transfers between devices  28.3 us (16%)
  local copies, waits for them, and re-layouts  15.6 us (9%)
  other arithmetic  6.78 us (4%)
  matrix products  3.7 us (2%)
    ppermute x3, waiting for transfers between devices, gather_blocks(): other = lax.ppermute(held, axis, [(i, i ^ step) for i in range(size)])  36.4 us
    all_gather x2, blocking collectives, gathered_sum(): return jnp.sum(lax.all_gather(x, axis), axis=0)  33.6 us
    all_gather x1, blocking collectives, per_device(): every_state = lax.all_gather(state, 'seq')  18.2 us
    ppermute x4, waiting for transfers between devices, butterfly_sum(): x = x + lax.ppermute(x, axis, pairs)  16.8 us
    ppermute x3, starting transfers between devices, gather_blocks(): other = lax.ppermute(held, axis, [(i, i ^ step) for i in range(size)])  14.9 us
    psum x1, blocking collectives, per_device(): projected = lax.psum(partial_output, 'tp').astype(jnp.bfloat16)  10.5 us
    unnamed x36, local copies, waits for them, and re-layouts  10.3 us
    ppermute x4, starting transfers between devices, butterfly_sum(): x = x + lax.ppermute(x, axis, pairs)  9.69 us
  transfers between devices with their start and end apart: 8, of which 7 were waited for; matrix products, arithmetic and copies ran while one was open for 12% of the time, Pallas kernels for 0%

profile of v1, /device:TPU:64, one launch (start us, length us, event | category | flops | bytes accessed | tf_op | source)
XLA Modules:
  0.0 177.1 jit_solution(13447083995003345248)
XLA Ops:
  0.7 1.0 reshape.181
  1.6 0.9 maximum_bitcast_fusion
  2.5 3.5 %collective-permute-start = (bf16[1,3,256,128]{3,2,1,0:T(8,128)(2,1)S(1)}, bf16[1,3,256,128]{3,2,1,0:T(8,128)(2,1)}, u32[]{:S(2)}, u32[]{:S(2)}) collective-permute-start(bf16[1,3,256,128]{3,2,1,0:T(8,128)(2,1)S(1)} %maximum_bitcast_fusion), channel_id=1, source_target_pairs={{0,4},{4,0},{8,12},{12,8},{16,20},{20,16},{24,28},{28,24},{1,5},{5... | collective-permute-start | bytes 589832 | tf_op jit(solution)/shard_map/mlp_weight_gather/ppermute | solution.py:46
  6.0 0.8 convert_element_type.73
  6.8 0.9 multiply_reduce_fusion.1
  7.7 0.8 dynamic-slice
  8.7 0.9 fusion.24
  9.6 0.9 fusion.28
  10.5 21.3 %all-gather = f32[128,768]{1,0:T(8,128)S(1)} all-gather(f32[8,768]{1,0:T(8,128)S(1)} %pad_maximum_fusion.1), channel_id=2, replica_groups=mesh['seq'=16,'mlp'=8,'tp'=4] {'seq'}, dimensions={0}, use_global_device_ids=true | all-gather | bytes 417792 | tf_op jit(solution)/shard_map/qkv_projection/all_gather | solution.py:37
  32.1 0.5 copy.107
  32.7 0.5 copy.110
  35.0 18.2 %all-gather.1 = f32[128,2,4,66]{3,2,1,0:T(4,128)S(1)} all-gather(f32[8,2,4,66]{3,2,1,0:T(4,128)S(1)} %pad_maximum_fusion), channel_id=3, replica_groups=mesh['seq'=16,'mlp'=8,'tp'=4] {'seq'}, dimensions={0}, use_global_device_ids=true | all-gather | bytes 287232 | tf_op jit(solution)/shard_map/softmax_merge/all_gather | solution.py:146
  54.9 0.5 copy.127
  56.5 10.5 %psum.7 = bf16[8,128]{1,0:T(8,128)(2,1)S(1)} all-reduce(f32[8,128]{1,0:T(8,128)S(1)} %fusion.30), channel_id=1, replica_groups=mesh['seq'=16,'mlp'=8,'tp'=4] {'tp'}, use_global_device_ids=true, to_apply=%region_8.9 | all-reduce | flops 1024 | bytes 6144 | tf_op jit(solution)/shard_map/output_projection/psum | solution.py:172
  67.0 0.6 constant_dynamic-update-slice_fusion.15
  67.6 0.6 constant_dynamic-update-slice_fusion.14
  68.2 0.6 constant_dynamic-update-slice_fusion.13
  68.8 0.6 constant_dynamic-update-slice_fusion.12
  69.3 0.6 constant_dynamic-update-slice_fusion.11
  69.9 0.6 constant_dynamic-update-slice_fusion.10
  70.5 0.6 constant_dynamic-update-slice_fusion.9
  71.1 0.6 constant_dynamic-update-slice_fusion.8
  71.7 1.1 maximum_select_fusion.2
  72.7 4.5 %collective-permute-start.1 = (bf16[2,3,256,128]{3,2,1,0:T(8,128)(2,1)S(1)}, bf16[2,3,256,128]{3,2,1,0:T(8,128)(2,1)S(1)}, u32[]{:S(2)}, u32[]{:S(2)}) collective-permute-start(bf16[2,3,256,128]{3,2,1,0:T(8,128)(2,1)S(1)} %maximum_select_fusion.2), channel_id=1, source_target_pairs={{0,8},{4,12},{8,0},{12,4},{16,24},{20,28},{24,16},{28,20},{1,9},{5... | collective-permute-start | bytes 1179656 | tf_op jit(solution)/shard_map/mlp_weight_gather/ppermute | solution.py:46
  77.2 0.6 constant_dynamic-update-slice_fusion.7
  77.8 0.6 constant_dynamic-update-slice_fusion.6
  78.4 0.6 constant_dynamic-update-slice_fusion.5
  79.0 0.6 constant_dynamic-update-slice_fusion.4
  79.6 13.6 %collective-permute-done.1 = bf16[2,3,256,128]{3,2,1,0:T(8,128)(2,1)S(1)} collective-permute-done((bf16[2,3,256,128]{3,2,1,0:T(8,128)(2,1)S(1)}, bf16[2,3,256,128]{3,2,1,0:T(8,128)(2,1)S(1)}, u32[]{:S(2)}, u32[]{:S(2)}) %collective-permute-start.1) | collective-permute-done | bytes 393248 | tf_op jit(solution)/shard_map/mlp_weight_gather/ppermute | solution.py:46
  93.3 6.9 %collective-permute-start.2 = (bf16[4,3,256,128]{3,2,1,0:T(8,128)(2,1)S(1)}, bf16[4,3,256,128]{3,2,1,0:T(8,128)(2,1)S(1)}, u32[]{:S(2)}, u32[]{:S(2)}) collective-permute-start(bf16[4,3,256,128]{3,2,1,0:T(8,128)(2,1)S(1)} %maximum_select_fusion.1), channel_id=1, source_target_pairs={{0,16},{4,20},{8,24},{12,28},{16,0},{20,4},{24,8},{28,12},{1,17},{... | collective-permute-start | bytes 2359304 | tf_op jit(solution)/shard_map/mlp_weight_gather/ppermute | solution.py:46
  100.3 0.6 constant_dynamic-update-slice_fusion.3
  100.9 0.6 constant_dynamic-update-slice_fusion.2
  101.4 0.6 constant_dynamic-update-slice_fusion.1
  102.0 0.6 constant_dynamic-update-slice_fusion
  102.6 3.6 %all-to-all-start = ((bf16[8,16,128]{2,0,1:T(8,128)(2,1)}), bf16[8,16,128]{2,0,1:T(8,128)(2,1)S(1)}, u32[]{:S(2)}, u32[]{:S(2)}) async-start(bf16[8,16,128]{2,0,1:T(8,128)(2,1)} %bitcast.11), calls=%async_computation | async-start | bytes 65536 | tf_op jit(solution)/shard_map/output_projection/all_to_all | solution.py:11
  106.3 6.3 %all-to-all-done = bf16[8,16,128]{2,0,1:T(8,128)(2,1)S(1)} async-done(((bf16[8,16,128]{2,0,1:T(8,128)(2,1)}), bf16[8,16,128]{2,0,1:T(8,128)(2,1)S(1)}, u32[]{:S(2)}, u32[]{:S(2)}) %all-to-all-start) | async-done | bytes 32800 | tf_op jit(solution)/shard_map/output_projection/all_to_all | solution.py:11
  112.7 22.8 %collective-permute-done.2 = bf16[4,3,256,128]{3,2,1,0:T(8,128)(2,1)S(1)} collective-permute-done((bf16[4,3,256,128]{3,2,1,0:T(8,128)(2,1)S(1)}, bf16[4,3,256,128]{3,2,1,0:T(8,128)(2,1)S(1)}, u32[]{:S(2)}, u32[]{:S(2)}) %collective-permute-start.2) | collective-permute-done | bytes 786464 | tf_op jit(solution)/shard_map/mlp_weight_gather/ppermute | solution.py:46
  137.0 12.3 %all-gather.2 = f32[32,2048]{1,0:T(8,128)S(1)} all-gather(f32[8,2048]{1,0:T(8,128)S(1)} %fusion.13), channel_id=4, replica_groups=mesh['seq'=16,'mlp'=8,'tp'=4] {'tp'}, dimensions={0}, use_global_device_ids=true | all-gather | bytes 327680 | tf_op jit(solution)/shard_map/down_reduction/all_gather | solution.py:37
  149.3 1.9 %collective-permute-start.3 = (f32[8,2048]{1,0:T(8,128)S(1)}, f32[8,2048]{1,0:T(8,128)S(1)}, u32[]{:S(2)}, u32[]{:S(2)}) collective-permute-start(f32[8,2048]{1,0:T(8,128)S(1)} %bitcast_reduce_fusion.1), channel_id=1, source_target_pairs={{0,32},{32,0},{64,96},{96,64},{128,160},{160,128},{192,224},{224,1... | collective-permute-start | bytes 196616 | tf_op jit(solution)/shard_map/down_reduction/ppermute | solution.py:60
  151.2 1.2 collective-permute-done.3
  152.4 2.3 %collective-permute-start.4 = (f32[8,2048]{1,0:T(8,128)S(1)}, f32[8,2048]{1,0:T(8,128)S(1)}, u32[]{:S(2)}, u32[]{:S(2)}) collective-permute-start(f32[8,2048]{1,0:T(8,128)S(1)} %add.98), channel_id=1, source_target_pairs={{0,64},{32,96},{64,0},{96,32},{128,192},{160,224},{192,128},{224,1... | collective-permute-start | bytes 196616 | tf_op jit(solution)/shard_map/down_reduction/ppermute | solution.py:60
  154.7 3.9 %collective-permute-done.4 = f32[8,2048]{1,0:T(8,128)S(1)} collective-permute-done((f32[8,2048]{1,0:T(8,128)S(1)}, f32[8,2048]{1,0:T(8,128)S(1)}, u32[]{:S(2)}, u32[]{:S(2)}) %collective-permute-start.4) | collective-permute-done | bytes 65568 | tf_op jit(solution)/shard_map/down_reduction/ppermute | solution.py:60
  158.6 2.2 %collective-permute-start.5 = (f32[8,2048]{1,0:T(8,128)S(1)}, f32[8,2048]{1,0:T(8,128)S(1)}, u32[]{:S(2)}, u32[]{:S(2)}) collective-permute-start(f32[8,2048]{1,0:T(8,128)S(1)} %add.99), channel_id=1, source_target_pairs={{0,128},{32,160},{64,192},{96,224},{128,0},{160,32},{192,64},{224,... | collective-permute-start | bytes 196616 | tf_op jit(solution)/shard_map/down_reduction/ppermute | solution.py:60
  160.8 4.9 %collective-permute-done.5 = f32[8,2048]{1,0:T(8,128)S(1)} collective-permute-done((f32[8,2048]{1,0:T(8,128)S(1)}, f32[8,2048]{1,0:T(8,128)S(1)}, u32[]{:S(2)}, u32[]{:S(2)}) %collective-permute-start.5) | collective-permute-done | bytes 65568 | tf_op jit(solution)/shard_map/down_reduction/ppermute | solution.py:60
  165.7 3.4 %collective-permute-start.6 = (f32[8,2048]{1,0:T(8,128)S(1)}, f32[8,2048]{1,0:T(8,128)S(1)}, u32[]{:S(2)}, u32[]{:S(2)}) collective-permute-start(f32[8,2048]{1,0:T(8,128)S(1)} %add.100), channel_id=1, source_target_pairs={{0,256},{32,288},{64,320},{96,352},{128,384},{160,416},{192,448},{... | collective-permute-start | bytes 196616 | tf_op jit(solution)/shard_map/down_reduction/ppermute | solution.py:60
  169.0 0.7 convert_element_type.92
  169.7 6.7 %collective-permute-done.6 = f32[8,2048]{1,0:T(8,128)S(1)} collective-permute-done((f32[8,2048]{1,0:T(8,128)S(1)}, f32[8,2048]{1,0:T(8,128)S(1)}, u32[]{:S(2)}, u32[]{:S(2)}) %collective-permute-start.6) | collective-permute-done | bytes 65568 | tf_op jit(solution)/shard_map/down_reduction/ppermute | solution.py:60
  176.5 0.6 add_convert_fusion
  (74 shorter events, 6.7 us)
Async XLA Ops:
  0.6 7.8 %copy-start = (bf16[128,512]{1,0:T(8,128)(2,1)S(1)}, bf16[128,512]{1,0:T(8,128)(2,1)}, u32[]{:S(2)}) copy-start(bf16[128,512]{1,0:T(8,128)(2,1)} %param.16) | copy-start | bytes 393220
  0.6 31.4 %copy-start.8 = (s32[8]{0:T(128)S(1)}, s32[8]{0:T(128)}, u32[]{:S(2)}) copy-start(s32[8]{0:T(128)} %param.14) | copy-start | bytes 100
  0.7 31.5 %copy-start.2 = (bf16[8,512,128]{2,1,0:T(8,128)(2,1)S(1)}, bf16[8,512,128]{2,1,0:T(8,128)(2,1)}, u32[]{:S(2)}) copy-start(bf16[8,512,128]{2,1,0:T(8,128)(2,1)} %param.19) | copy-start | bytes 3145732
  2.5 69.1 %collective-permute-start = (bf16[1,3,256,128]{3,2,1,0:T(8,128)(2,1)S(1)}, bf16[1,3,256,128]{3,2,1,0:T(8,128)(2,1)}, u32[]{:S(2)}, u32[]{:S(2)}) collective-permute-start(bf16[1,3,256,128]{3,2,1,0:T(8,128)(2,1)S(1)} %maximum_bitcast_fusion), channel_id=1, source_target_pairs={{0,4},{4,0},{8,12},{12,8},{16,20},{20,16},{24,28},{28,24},{1,5},{5... | collective-permute-start | bytes 589832 | tf_op jit(solution)/shard_map/mlp_weight_gather/ppermute | solution.py:46
  10.5 22.1 %copy-start.3 = (bf16[8,512,128]{2,1,0:T(8,128)(2,1)S(1)}, bf16[8,512,128]{2,1,0:T(8,128)(2,1)}, u32[]{:S(2)}) copy-start(bf16[8,512,128]{2,1,0:T(8,128)(2,1)} %param.20) | copy-start | bytes 3145732
  31.9 1.3 copy-start.5
  31.9 24.2 %copy-start.6 = (bf16[8,128]{1,0:T(8,128)(2,1)}, bf16[8,128]{1,0:T(8,128)(2,1)S(1)}, u32[]{:S(2)}) copy-start(bf16[8,128]{1,0:T(8,128)(2,1)S(1)} %slice.79) | copy-start | bytes 6148
  53.2 0.7 slice-start
  53.9 2.5 %copy-start.4 = (bf16[512,128]{1,0:T(8,128)(2,1)S(1)}, bf16[512,128]{1,0:T(8,128)(2,1)}, u32[]{:S(2)}) copy-start(bf16[512,128]{1,0:T(8,128)(2,1)} %param.21) | copy-start | bytes 393220
  56.1 50.1 %copy-start.7 = (bf16[2048]{0:T(1024)(128)(2,1)S(1)}, bf16[2048]{0:T(1024)(128)(2,1)}, u32[]{:S(2)}) copy-start(bf16[2048]{0:T(1024)(128)(2,1)} %param.22) | copy-start | bytes 12292
  56.1 56.5 %copy-start.1 = (bf16[8,2048]{1,0:T(8,128)(2,1)S(1)}, bf16[8,2048]{1,0:T(8,128)(2,1)}, u32[]{:S(2)}) copy-start(bf16[8,2048]{1,0:T(8,128)(2,1)} %param.13) | copy-start | bytes 98308
  72.7 20.5 %collective-permute-start.1 = (bf16[2,3,256,128]{3,2,1,0:T(8,128)(2,1)S(1)}, bf16[2,3,256,128]{3,2,1,0:T(8,128)(2,1)S(1)}, u32[]{:S(2)}, u32[]{:S(2)}) collective-permute-start(bf16[2,3,256,128]{3,2,1,0:T(8,128)(2,1)S(1)} %maximum_select_fusion.2), channel_id=1, source_target_pairs={{0,8},{4,12},{8,0},{12,4},{16,24},{20,28},{24,16},{28,20},{1,9},{5... | collective-permute-start | bytes 1179656 | tf_op jit(solution)/shard_map/mlp_weight_gather/ppermute | solution.py:46
  93.3 42.2 %collective-permute-start.2 = (bf16[4,3,256,128]{3,2,1,0:T(8,128)(2,1)S(1)}, bf16[4,3,256,128]{3,2,1,0:T(8,128)(2,1)S(1)}, u32[]{:S(2)}, u32[]{:S(2)}) collective-permute-start(bf16[4,3,256,128]{3,2,1,0:T(8,128)(2,1)S(1)} %maximum_select_fusion.1), channel_id=1, source_target_pairs={{0,16},{4,20},{8,24},{12,28},{16,0},{20,4},{24,8},{28,12},{1,17},{... | collective-permute-start | bytes 2359304 | tf_op jit(solution)/shard_map/mlp_weight_gather/ppermute | solution.py:46
  102.6 10.0 %all-to-all-start = ((bf16[8,16,128]{2,0,1:T(8,128)(2,1)}), bf16[8,16,128]{2,0,1:T(8,128)(2,1)S(1)}, u32[]{:S(2)}, u32[]{:S(2)}) async-start(bf16[8,16,128]{2,0,1:T(8,128)(2,1)} %bitcast.11), calls=%async_computation | async-start | bytes 65536 | tf_op jit(solution)/shard_map/output_projection/all_to_all | solution.py:11
  149.3 3.1 %collective-permute-start.3 = (f32[8,2048]{1,0:T(8,128)S(1)}, f32[8,2048]{1,0:T(8,128)S(1)}, u32[]{:S(2)}, u32[]{:S(2)}) collective-permute-start(f32[8,2048]{1,0:T(8,128)S(1)} %bitcast_reduce_fusion.1), channel_id=1, source_target_pairs={{0,32},{32,0},{64,96},{96,64},{128,160},{160,128},{192,224},{224,1... | collective-permute-start | bytes 196616 | tf_op jit(solution)/shard_map/down_reduction/ppermute | solution.py:60
  152.4 6.2 %collective-permute-start.4 = (f32[8,2048]{1,0:T(8,128)S(1)}, f32[8,2048]{1,0:T(8,128)S(1)}, u32[]{:S(2)}, u32[]{:S(2)}) collective-permute-start(f32[8,2048]{1,0:T(8,128)S(1)} %add.98), channel_id=1, source_target_pairs={{0,64},{32,96},{64,0},{96,32},{128,192},{160,224},{192,128},{224,1... | collective-permute-start | bytes 196616 | tf_op jit(solution)/shard_map/down_reduction/ppermute | solution.py:60
  158.6 7.1 %collective-permute-start.5 = (f32[8,2048]{1,0:T(8,128)S(1)}, f32[8,2048]{1,0:T(8,128)S(1)}, u32[]{:S(2)}, u32[]{:S(2)}) collective-permute-start(f32[8,2048]{1,0:T(8,128)S(1)} %add.99), channel_id=1, source_target_pairs={{0,128},{32,160},{64,192},{96,224},{128,0},{160,32},{192,64},{224,... | collective-permute-start | bytes 196616 | tf_op jit(solution)/shard_map/down_reduction/ppermute | solution.py:60
  165.7 10.8 %collective-permute-start.6 = (f32[8,2048]{1,0:T(8,128)S(1)}, f32[8,2048]{1,0:T(8,128)S(1)}, u32[]{:S(2)}, u32[]{:S(2)}) collective-permute-start(f32[8,2048]{1,0:T(8,128)S(1)} %add.100), channel_id=1, source_target_pairs={{0,256},{32,288},{64,320},{96,352},{128,384},{160,416},{192,448},{... | collective-permute-start | bytes 196616 | tf_op jit(solution)/shard_map/down_reduction/ppermute | solution.py:60
